TPU v7x, 128 devices: a whole 4x4x4 slice. The times are simulated.
128 devices in a mesh: ma: 16 (over x, z), band: 8 (over y, core).
Axes of the slice: x: 4, y: 4, z: 4, core: 2. Of those that a mesh axis runs over, the one named last changes fastest.
Arguments:
- harmonics: bfloat16 [128, 8192, 256], P(('ma', 'band')), may hold values from -6 to 6
- legendre: bfloat16 [128, 2, 8192, 512], P(('ma', 'band')), may hold values from -0.0029296875 to 0.0029296875
- m_values: int32 [128], replicated, may hold values from 1 to 8191
- cycle_cell: int32 [16384], P(('ma', 'band')), may hold values from 0 to 63, as said below
- phi_cell: int32 [16384], P(('ma', 'band')), may hold values from 3 to 123
- offsets: float32 [2, 16384], P(None, ('ma', 'band')), may hold values from 0 to 1
Outputs:
- lensed: float32 [16384, 128], P(('ma', 'band'))
Inputs may be any that keep to these rules, and one draw needn't show every extreme that they name: `cycle_cell`: Band-local cycle; every point held by device (ma, band) lies in latitude band `band`. For each device and each ma index q, at most 16 of its points have cycles q * 4 to q * 4 + 3, and in every band one q receives exactly 16 points from every device of the band.
All inputs are finite; a program needn't handle non-finite values.
Results may differ from a plain program's by a relative error of at most 0.0053.
Values may be sent and summed in bfloat16 or wider, within the bound.
No kernel may reach another device: no remote copies, remote signals or barrier semaphores. Data moves between devices by JAX's collectives and lax.ppermute only.
A program may use at most 64 MiB of HBM per device.

v0:
```python
import jax
import jax.numpy as jnp
from jax import lax
from jax.sharding import PartitionSpec as P

NPHI = 128


def with_halo(x, sides, width):
    for axis, dim in sides:
        count, length = (lax.axis_size(axis), x.shape[dim])
        up = [(i, (i + 1) % count) for i in range(count - 1)]
        down = [(j, i) for i, j in up]
        last = lax.slice_in_dim(x, length - width, length, axis=dim)
        first = lax.slice_in_dim(x, 0, width, axis=dim)
        before = lax.ppermute(last, axis, up)
        after = lax.ppermute(first, axis, down)
        x = jnp.concatenate([before, x, after], axis=dim)
    return x


def kernel_taps(shifts):
    return jnp.sinc(shifts) * jnp.sinc(shifts / 4.0)


def combine_parts(plus_part, minus_part):
    q_real = -(plus_part[:, 0, 0] - minus_part[:, 1, 1])
    q_imag = -(plus_part[:, 0, 1] + minus_part[:, 1, 0])
    u_real = -(plus_part[:, 1, 0] + minus_part[:, 0, 1])
    u_imag = -(plus_part[:, 1, 1] - minus_part[:, 0, 0])
    real_part = jnp.concatenate([q_real, u_real], axis=1)
    imag_part = jnp.concatenate([q_imag, u_imag], axis=1)
    return jnp.stack([real_part, imag_part], axis=1).astype(jnp.bfloat16)


def phase_table(m_values, cell_count, lmax_width):
    pixel_index = jnp.arange(cell_count, dtype=jnp.int32)
    period = 2 * lmax_width
    phase_turns = m_values[None, :] * pixel_index[:, None] % period
    angles = phase_turns.astype(jnp.float32) * (2.0 * jnp.pi / period)
    return jnp.stack([jnp.cos(angles), -jnp.sin(angles)], axis=-1).astype(jnp.bfloat16)


def spectral_cycles(phase_rows, spectra):
    summed = jnp.einsum("kmi,mric->rkc", phase_rows, spectra, preferred_element_type=jnp.float32)
    return (2.0 * summed).astype(jnp.bfloat16)


def spread_weights(starts, weights, length):
    tap_index = jnp.arange(8, dtype=jnp.int32)
    target = starts[:, None] + tap_index[None, :]
    cells = jnp.arange(length, dtype=jnp.int32)
    hits = (target[:, :, None] == cells[None, None, :]).astype(jnp.float32)
    return jnp.sum(weights[:, :, None] * hits, axis=1)


def on_device(harmonics, legendre, m_values, cycle_cell, phi_cell, offsets):
    evolutions = harmonics.shape[2] // 4
    cycle_total = legendre.shape[3]
    contract = (((0,), (0,)), ((), ()))
    plus_part = lax.dot_general(
        legendre[0, 0], harmonics[0], contract, preferred_element_type=jnp.float32
    )
    minus_part = lax.dot_general(
        legendre[0, 1], harmonics[0], contract, preferred_element_type=jnp.float32
    )
    spectra = combine_parts(
        plus_part.reshape(cycle_total, 2, 2, evolutions),
        minus_part.reshape(cycle_total, 2, 2, evolutions),
    )
    width_out = spectra.shape[2]
    owner_count = lax.axis_size("ma")
    band_count = lax.axis_size("band")
    cycle_depth = cycle_total // (owner_count * band_count)
    received = lax.all_to_all(
        spectra[None], ("ma", "band"), split_axis=1, concat_axis=0, tiled=True
    )
    phase_rows = phase_table(m_values, NPHI, harmonics.shape[1])
    own_grid = spectral_cycles(phase_rows, received)
    extended = with_halo(own_grid, (("ma", 0),), 4)
    ext_rows = extended.shape[0]
    flat_grid = extended.reshape(ext_rows * NPHI, width_out)
    first_cycle = lax.axis_index("ma") * cycle_depth
    capacity = cycle_cell.shape[0] // 8
    owner_index = cycle_cell // cycle_depth
    one_hot = (owner_index[:, None] == jnp.arange(owner_count, dtype=jnp.int32)[None, :]).astype(
        jnp.int32
    )
    slot_index = jnp.sum((jnp.cumsum(one_hot, axis=0) - one_hot) * one_hot, axis=1)
    flat_slot = owner_index * capacity + slot_index
    placement = (
        flat_slot[:, None] == jnp.arange(owner_count * capacity, dtype=jnp.int32)[None, :]
    ).astype(jnp.float32)
    point_table = jnp.stack(
        [cycle_cell.astype(jnp.float32), phi_cell.astype(jnp.float32), offsets[0], offsets[1]],
        axis=1,
    )
    buffers = jnp.dot(placement.T, point_table, precision=lax.Precision.HIGHEST).reshape(
        owner_count, capacity, 4
    )
    cycle_buffer = buffers[:, :, 0].astype(jnp.int32)
    phi_buffer = buffers[:, :, 1].astype(jnp.int32)
    offset_buffer = buffers[:, :, 2:4]
    cycles_here = lax.all_to_all(cycle_buffer, "ma", split_axis=0, concat_axis=0, tiled=True)
    phis_here = lax.all_to_all(phi_buffer, "ma", split_axis=0, concat_axis=0, tiled=True)
    offsets_here = lax.all_to_all(offset_buffer, "ma", split_axis=0, concat_axis=0, tiled=True)
    sources, items = cycles_here.shape
    cycles_flat = cycles_here.reshape(-1)
    phis_flat = phis_here.reshape(-1)
    pairs = offsets_here.reshape(-1, 2)
    tap_shift = jnp.arange(8).astype(jnp.float32) - 3.0
    across = kernel_taps(tap_shift[None, :] - pairs[:, 0:1])
    beside_all = kernel_taps(tap_shift[None, :] - pairs[:, 1:2])
    cycle_weights = spread_weights(cycles_flat + 1 - first_cycle, across, ext_rows)
    phi_weights = spread_weights(phis_flat - 3, beside_all, NPHI)
    dense = (cycle_weights[:, :, None] * phi_weights[:, None, :]).astype(jnp.bfloat16)
    dense = dense.reshape(cycles_flat.shape[0], ext_rows * NPHI)
    values = jnp.dot(dense, flat_grid, preferred_element_type=jnp.float32)
    values = values.reshape(sources, items, width_out)
    returned = lax.all_to_all(values, "ma", split_axis=0, concat_axis=0, tiled=True)
    return jnp.dot(
        placement,
        returned.reshape(owner_count * capacity, width_out),
        precision=lax.Precision.HIGHEST,
    )


def solution(mesh):
    in_specs = (
        P(("ma", "band"), None, None),
        P(("ma", "band"), None, None, None),
        P(),
        P(("ma", "band")),
        P(("ma", "band")),
        P(None, ("ma", "band")),
    )
    out_specs = P(("ma", "band"), None)
    return jax.shard_map(
        on_device, mesh=mesh, in_specs=in_specs, out_specs=out_specs, check_vma=False
    )
```

profile of v0, /device:TPU:0, one launch (start us, length us, event | category | flops | bytes accessed | tf_op | source)
XLA Modules:
  0.0 100.5 jit_solution(4948932564756850836)
XLA Ops:
  0.0 0.7 convert_bitcast_fusion.1
  0.8 0.2 reduce_window_sum.11
  1.0 0.2 select_reduce_fusion.2
  1.2 0.8 slice_bitcast_fusion.1
  2.0 0.7 convert_bitcast_fusion
  2.6 0.2 fusion.19
  2.9 0.6 slice_convert_fusion.1
  3.5 8.0 %all-to-all-start = ((s32[16,1,16]{2,1,0:T(1,128)}), s32[16,1,16]{2,1,0:T(1,128)S(1)}, u32[]{:S(2)}, u32[]{:S(2)}) async-start(s32[16,1,16]{2,1,0:T(1,128)} %bitcast.4), calls=%async_computation | async-start | bytes 16384 | tf_op jit(solution)/shard_map/all_to_all | solution.py:104
  11.5 6.4 %copy.40 = bf16[1,8192,256]{1,2,0:T(8,128)(2,1)} copy(bf16[1,8192,256]{2,1,0:T(8,128)(2,1)} %param.7) | data formatting | bytes 8388608 | tf_op args[0]
  17.9 7.0 %fusion = f32[512,2,2,64]{0,3,2,1:T(8,128)S(1)} fusion(bf16[2,2,64,8192]{3,2,1,0:T(8,128)(2,1)} %bitcast.73, bf16[1,2,8192,512]{3,2,1,0:T(8,128)(2,1)} %param.8), kind=kOutput, calls=%fused_computation | convolution fusion | flops 2147483648 | bytes 13107200 | tf_op jit(solution)/shard_map/dot_general | solution.py:64
  25.0 3.6 %copy-done.2 = bf16[1,2,8192,512]{3,2,1,0:T(8,128)(2,1)S(1)} copy-done((bf16[1,2,8192,512]{3,2,1,0:T(8,128)(2,1)S(1)}, bf16[1,2,8192,512]{3,2,1,0:T(8,128)(2,1)}, u32[]{:S(2)}) %copy-start.2) | copy-done | bytes 16777240
  28.5 2.3 %fusion.2 = f32[512,2,2,64]{0,3,2,1:T(8,128)S(1)} fusion(bf16[2,2,64,8192]{3,2,1,0:T(8,128)(2,1)S(1)} %bitcast.74, bf16[1,2,8192,512]{3,2,1,0:T(8,128)(2,1)S(1)} %copy-done.2), kind=kOutput, calls=%fused_computation.2 | convolution fusion | flops 2147483648 | bytes 13107200 | tf_op jit(solution)/shard_map/dot_general | solution.py:61
  30.9 0.3 cosine_convert_fusion
  31.4 7.2 %all-to-all-start.2 = ((s32[16,1,16]{2,1,0:T(1,128)}), s32[16,1,16]{2,1,0:T(1,128)S(1)}, u32[]{:S(2)}, u32[]{:S(2)}) async-start(s32[16,1,16]{2,1,0:T(1,128)} %bitcast.7), calls=%async_computation.2 | async-start | bytes 16384 | tf_op jit(solution)/shard_map/all_to_all | solution.py:105
  38.6 0.9 copy.41
  39.5 0.6 copy.35
  40.1 6.1 %all-to-all-done.2 = s32[16,1,16]{2,1,0:T(1,128)S(1)} async-done(((s32[16,1,16]{2,1,0:T(1,128)}), s32[16,1,16]{2,1,0:T(1,128)S(1)}, u32[]{:S(2)}, u32[]{:S(2)}) %all-to-all-start.2) | async-done | bytes 1056 | tf_op jit(solution)/shard_map/all_to_all | solution.py:105
  46.2 3.5 %all-to-all-start.1 = ((f32[16,16,2]{1,2,0:T(2,128)}), f32[16,16,2]{1,2,0:T(2,128)S(1)}, u32[]{:S(2)}, u32[]{:S(2)}) async-start(f32[16,16,2]{1,2,0:T(2,128)} %copy.35), calls=%async_computation.1 | async-start | bytes 32768 | tf_op jit(solution)/shard_map/all_to_all | solution.py:106
  50.0 7.2 %all-to-all-done.1 = f32[16,16,2]{1,2,0:T(2,128)S(1)} async-done(((f32[16,16,2]{1,2,0:T(2,128)}), f32[16,16,2]{1,2,0:T(2,128)S(1)}, u32[]{:S(2)}, u32[]{:S(2)}) %all-to-all-start.1) | async-done | bytes 2080 | tf_op jit(solution)/shard_map/all_to_all | solution.py:106
  57.2 6.4 %all-to-all-start.3 = ((bf16[1,512,2,128]{3,2,0,1:T(2,128)(2,1)}), bf16[1,512,2,128]{3,2,0,1:T(2,128)(2,1)S(1)}, u32[]{:S(2)}, u32[]{:S(2)}) async-start(bf16[1,512,2,128]{3,2,0,1:T(2,128)(2,1)} %copy.41), calls=%async_computation.3 | async-start | bytes 524288 | tf_op jit(solution)/shard_map/all_to_all | solution.py:75
  64.0 0.1 copy.39
  64.2 1.3 %select_reduce_fusion = f32[256,128]{1,0:T(8,128)S(1)} fusion(f32[256,8]{1,0:T(8,128)S(1)} %copy.39, s32[256,8]{1,0:T(8,128)S(1)} %iota_add_fusion), kind=kLoop, calls=%fused_computation.11 | loop fusion | flops 753664 | bytes 147456 | tf_op jit(solution)/shard_map/reduce_sum | solution.py:54
  65.4 8.9 %all-to-all-done.3 = bf16[1,512,2,128]{3,2,0,1:T(2,128)(2,1)S(1)} async-done(((bf16[1,512,2,128]{3,2,0,1:T(2,128)(2,1)}), bf16[1,512,2,128]{3,2,0,1:T(2,128)(2,1)S(1)}, u32[]{:S(2)}, u32[]{:S(2)}) %all-to-all-start.3) | async-done | bytes 262176 | tf_op jit(solution)/shard_map/all_to_all | solution.py:75
  74.4 0.2 fusion.8
  74.6 2.7 %collective-permute-start = (bf16[4,128,128]{2,1,0:T(8,128)(2,1)S(1)}, bf16[4,128,128]{2,1,0:T(8,128)(2,1)S(1)}, u32[]{:S(2)}, u32[]{:S(2)}) collective-permute-start(bf16[4,128,128]{2,1,0:T(8,128)(2,1)S(1)} %fusion.8), channel_id=1, source_target_pairs={{0,8},{8,16},{16,24},{24,32},{32,40},{40,48},{48,56},{56,64},{64,7... | collective-permute-start | bytes 393224 | tf_op jit(solution)/shard_map/ppermute | solution.py:16
  77.3 1.3 %collective-permute-start.1 = (bf16[4,128,128]{2,1,0:T(8,128)(2,1)S(1)}, bf16[4,128,128]{2,1,0:T(8,128)(2,1)S(1)}, u32[]{:S(2)}, u32[]{:S(2)}) collective-permute-start(bf16[4,128,128]{2,1,0:T(8,128)(2,1)S(1)} %fusion.8), channel_id=1, source_target_pairs={{8,0},{16,8},{24,16},{32,24},{40,32},{48,40},{56,48},{64,56},{72,6... | collective-permute-start | bytes 393224 | tf_op jit(solution)/shard_map/ppermute | solution.py:17
  78.6 0.7 multiply_convert_fusion
  79.3 0.5 convert_element_type.102
  79.9 4.3 %collective-permute-done.1 = bf16[4,128,128]{2,1,0:T(8,128)(2,1)S(1)} collective-permute-done((bf16[4,128,128]{2,1,0:T(8,128)(2,1)S(1)}, bf16[4,128,128]{2,1,0:T(8,128)(2,1)S(1)}, u32[]{:S(2)}, u32[]{:S(2)}) %collective-permute-start.1) | collective-permute-done | bytes 131104 | tf_op jit(solution)/shard_map/ppermute | solution.py:17
  84.2 0.4 fusion.131
  84.6 15.0 %all_to_all.34 = f32[16,16,128]{2,1,0:T(8,128)S(1)} all-to-all(f32[16,16,128]{2,1,0:T(8,128)S(1)} %fusion.131), channel_id=1, replica_groups=mesh['ma'=16,'band'=8] {'ma'}, dimensions={0} | all-to-all | bytes 262144 | tf_op jit(solution)/shard_map/all_to_all | solution.py:120
  99.6 0.9 fusion.18
  (27 shorter events, 1.1 us)
Async XLA Ops:
  3.5 27.8 %all-to-all-start = ((s32[16,1,16]{2,1,0:T(1,128)}), s32[16,1,16]{2,1,0:T(1,128)S(1)}, u32[]{:S(2)}, u32[]{:S(2)}) async-start(s32[16,1,16]{2,1,0:T(1,128)} %bitcast.4), calls=%async_computation | async-start | bytes 16384 | tf_op jit(solution)/shard_map/all_to_all | solution.py:104
  17.9 7.1 %copy-start = (bf16[1,8192,256]{1,2,0:T(8,128)(2,1)S(1)}, bf16[1,8192,256]{1,2,0:T(8,128)(2,1)}, u32[]{:S(2)}) copy-start(bf16[1,8192,256]{1,2,0:T(8,128)(2,1)} %copy.40) | copy-start | bytes 12582916
  17.9 10.6 %copy-start.2 = (bf16[1,2,8192,512]{3,2,1,0:T(8,128)(2,1)S(1)}, bf16[1,2,8192,512]{3,2,1,0:T(8,128)(2,1)}, u32[]{:S(2)}) copy-start(bf16[1,2,8192,512]{3,2,1,0:T(8,128)(2,1)} %param.8) | copy-start | bytes 50331652
  28.5 2.3 %copy-start.1 = (s32[128]{0:T(128)S(1)}, s32[128]{0:T(128)}, u32[]{:S(2)}) copy-start(s32[128]{0:T(128)} %param.9) | copy-start | bytes 1540
  31.4 14.8 %all-to-all-start.2 = ((s32[16,1,16]{2,1,0:T(1,128)}), s32[16,1,16]{2,1,0:T(1,128)S(1)}, u32[]{:S(2)}, u32[]{:S(2)}) async-start(s32[16,1,16]{2,1,0:T(1,128)} %bitcast.7), calls=%async_computation.2 | async-start | bytes 16384 | tf_op jit(solution)/shard_map/all_to_all | solution.py:105
  46.2 11.0 %all-to-all-start.1 = ((f32[16,16,2]{1,2,0:T(2,128)}), f32[16,16,2]{1,2,0:T(2,128)S(1)}, u32[]{:S(2)}, u32[]{:S(2)}) async-start(f32[16,16,2]{1,2,0:T(2,128)} %copy.35), calls=%async_computation.1 | async-start | bytes 32768 | tf_op jit(solution)/shard_map/all_to_all | solution.py:106
  57.2 17.2 %all-to-all-start.3 = ((bf16[1,512,2,128]{3,2,0,1:T(2,128)(2,1)}), bf16[1,512,2,128]{3,2,0,1:T(2,128)(2,1)S(1)}, u32[]{:S(2)}, u32[]{:S(2)}) async-start(bf16[1,512,2,128]{3,2,0,1:T(2,128)(2,1)} %copy.41), calls=%async_computation.3 | async-start | bytes 524288 | tf_op jit(solution)/shard_map/all_to_all | solution.py:75
  74.6 5.3 %collective-permute-start = (bf16[4,128,128]{2,1,0:T(8,128)(2,1)S(1)}, bf16[4,128,128]{2,1,0:T(8,128)(2,1)S(1)}, u32[]{:S(2)}, u32[]{:S(2)}) collective-permute-start(bf16[4,128,128]{2,1,0:T(8,128)(2,1)S(1)} %fusion.8), channel_id=1, source_target_pairs={{0,8},{8,16},{16,24},{24,32},{32,40},{40,48},{48,56},{56,64},{64,7... | collective-permute-start | bytes 393224 | tf_op jit(solution)/shard_map/ppermute | solution.py:16
  77.3 6.9 %collective-permute-start.1 = (bf16[4,128,128]{2,1,0:T(8,128)(2,1)S(1)}, bf16[4,128,128]{2,1,0:T(8,128)(2,1)S(1)}, u32[]{:S(2)}, u32[]{:S(2)}) collective-permute-start(bf16[4,128,128]{2,1,0:T(8,128)(2,1)S(1)} %fusion.8), channel_id=1, source_target_pairs={{8,0},{16,8},{24,16},{32,24},{40,32},{48,40},{56,48},{64,56},{72,6... | collective-permute-start | bytes 393224 | tf_op jit(solution)/shard_map/ppermute | solution.py:17
where the time goes:
time: 101 us
  starting transfers between devices  29.2 us (29%)
  waiting for transfers between devices  26.5 us (26%)
  blocking collectives  15 us (15%)
  local copies, waits for them, and re-layouts  13.3 us (13%)
  matrix products  11 us (11%)
  other arithmetic  5.22 us (5%)
    all_to_all x1, blocking collectives, on_device(): lax.all_to_all(values, 'ma', split_axis=0, concat_axis=0, tiled=True)  15 us
    unnamed x7, local copies, waits for them, and re-layouts  9.96 us
    all_to_all x1, waiting for transfers between devices, on_device(): lax.all_to_all(spectra[None], ('ma', 'band'), split_axis=1, concat_axis=0...  8.95 us
    all_to_all x1, starting transfers between devices, on_device(): lax.all_to_all(cycle_buffer, 'ma', split_axis=0, concat_axis=0, tiled=True)  7.99 us
    all_to_all x1, starting transfers between devices, on_device(): lax.all_to_all(phi_buffer, 'ma', split_axis=0, concat_axis=0, tiled=True)  7.22 us
    all_to_all x1, waiting for transfers between devices, on_device(): lax.all_to_all(offset_buffer, 'ma', split_axis=0, concat_axis=0, tiled=True)  7.19 us
    dot_general x1, matrix products, on_device(): lax.dot_general(legendre[0, 1], harmonics[0], contract, preferred_element...  7.04 us
    all_to_all x1, starting transfers between devices, on_device(): lax.all_to_all(spectra[None], ('ma', 'band'), split_axis=1, concat_axis=0...  6.44 us
  transfers between devices with their start and end apart: 6, of which 4 were waited for; matrix products, arithmetic and copies ran while one was open for 21% of the time, Pallas kernels for 0%

commit v1 on v0

--- a/solution.py
+++ b/solution.py
@@ -72,9 +72,10 @@
     owner_count = lax.axis_size("ma")
     band_count = lax.axis_size("band")
     cycle_depth = cycle_total // (owner_count * band_count)
-    received = lax.all_to_all(
-        spectra[None], ("ma", "band"), split_axis=1, concat_axis=0, tiled=True
-    )
+    value = spectra[None]
+    pieces = jnp.split(value, lax.axis_size(("ma", "band")), axis=1)
+    got = lax.all_to_all(jnp.stack(pieces), ("ma", "band"), 0, 0)
+    received = jnp.concatenate(got, axis=0)
     phase_rows = phase_table(m_values, NPHI, harmonics.shape[1])
     own_grid = spectral_cycles(phase_rows, received)
     extended = with_halo(own_grid, (("ma", 0),), 4)

time: 101 us -> 195 us (1.93)
  other arithmetic: 5.22 us -> 95.4 us
  local copies, waits for them, and re-layouts: 13.3 us -> 19.5 us
  waiting for transfers between devices: 26.5 us -> 20.5 us
  starting transfers between devices: 29.2 us -> 32.9 us
    unnamed x0 -> x127, other arithmetic: none -> 89.4 us
    another operation x1, local copies, waits for them, and re-layouts: 0.86 us -> 7.01 us  [on_device(): got = lax.all_to_all(jnp.stack(pieces), ('ma', 'band'), 0, 0)]
    all_to_all x1, waiting for transfers between devices: 6.09 us -> 0.01 us  [on_device(): lax.all_to_all(phi_buffer, 'ma', split_axis=0, concat_axis=0, tiled=True)]
    all_to_all x1, starting transfers between devices: 3.5 us -> 7.21 us  [on_device(): lax.all_to_all(offset_buffer, 'ma', split_axis=0, concat_axis=0, tiled=True)]
    unnamed x7 -> x9, local copies, waits for them, and re-layouts: 9.96 us -> 9.98 us
  transfers between devices with their start and end apart: 6 -> 6, of which waited for: 4 -> 3; matrix products, arithmetic and copies ran while one was open for 21% -> 60% of each run, Pallas kernels for 0% -> 0%
where the time goes in v1:
time: 195 us
  other arithmetic  95.4 us (49%)
  starting transfers between devices  32.9 us (17%)
  waiting for transfers between devices  20.5 us (11%)
  local copies, waits for them, and re-layouts  19.5 us (10%)
  blocking collectives  15 us (8%)
  matrix products  11 us (6%)
    unnamed x127, other arithmetic  89.4 us
    all_to_all x1, blocking collectives, on_device(): lax.all_to_all(values, 'ma', split_axis=0, concat_axis=0, tiled=True)  15 us
    unnamed x9, local copies, waits for them, and re-layouts  9.98 us
    all_to_all x1, waiting for transfers between devices, on_device(): got = lax.all_to_all(jnp.stack(pieces), ('ma', 'band'), 0, 0)  8.95 us
    all_to_all x1, starting transfers between devices, on_device(): lax.all_to_all(cycle_buffer, 'ma', split_axis=0, concat_axis=0, tiled=True)  7.99 us
    all_to_all x1, waiting for transfers between devices, on_device(): lax.all_to_all(offset_buffer, 'ma', split_axis=0, concat_axis=0, tiled=True)  7.26 us
    all_to_all x1, starting transfers between devices, on_device(): lax.all_to_all(phi_buffer, 'ma', split_axis=0, concat_axis=0, tiled=True)  7.21 us
    all_to_all x1, starting transfers between devices, on_device(): lax.all_to_all(offset_buffer, 'ma', split_axis=0, concat_axis=0, tiled=True)  7.21 us
  transfers between devices with their start and end apart: 6, of which 3 were waited for; matrix products, arithmetic and copies ran while one was open for 60% of the time, Pallas kernels for 0%

profile of v1, /device:TPU:0, one launch (start us, length us, event | category | flops | bytes accessed | tf_op | source)
XLA Modules:
  0.0 194.5 jit_solution(14473610986437217938)
XLA Ops:
  0.0 0.7 convert_bitcast_fusion.1
  1.2 0.8 slice_bitcast_fusion.1
  3.5 8.0 %all-to-all-start = ((s32[16,1,16]{2,1,0:T(1,128)}), s32[16,1,16]{2,1,0:T(1,128)S(1)}, u32[]{:S(2)}, u32[]{:S(2)}) async-start(s32[16,1,16]{2,1,0:T(1,128)} %bitcast.4), calls=%async_computation | async-start | bytes 16384 | tf_op jit(solution)/shard_map/all_to_all | solution.py:105
  11.5 6.4 %copy.292 = bf16[1,8192,256]{1,2,0:T(8,128)(2,1)} copy(bf16[1,8192,256]{2,1,0:T(8,128)(2,1)} %param.7) | data formatting | bytes 8388608 | tf_op args[0]
  17.9 7.0 %fusion = f32[512,2,2,64]{0,3,2,1:T(8,128)S(1)} fusion(bf16[2,2,64,8192]{3,2,1,0:T(8,128)(2,1)} %bitcast.587, bf16[1,2,8192,512]{3,2,1,0:T(8,128)(2,1)} %param.8), kind=kOutput, calls=%fused_computation | convolution fusion | flops 2147483648 | bytes 13107200 | tf_op jit(solution)/shard_map/dot_general | solution.py:64
  25.0 3.6 %copy-done.3 = bf16[1,2,8192,512]{3,2,1,0:T(8,128)(2,1)S(1)} copy-done((bf16[1,2,8192,512]{3,2,1,0:T(8,128)(2,1)S(1)}, bf16[1,2,8192,512]{3,2,1,0:T(8,128)(2,1)}, u32[]{:S(2)}) %copy-start.3) | copy-done | bytes 16777240
  28.6 2.3 %fusion.2 = f32[512,2,2,64]{0,3,2,1:T(8,128)S(1)} fusion(bf16[2,2,64,8192]{3,2,1,0:T(8,128)(2,1)S(1)} %bitcast.588, bf16[1,2,8192,512]{3,2,1,0:T(8,128)(2,1)S(1)} %copy-done.3), kind=kOutput, calls=%fused_computation.2 | convolution fusion | flops 2147483648 | bytes 13107200 | tf_op jit(solution)/shard_map/dot_general | solution.py:61
  33.1 0.7 constant_dynamic-update-slice_fusion.124
  35.2 0.7 constant_dynamic-update-slice_fusion.121
  40.2 0.7 constant_dynamic-update-slice_fusion.114
  49.4 0.7 constant_dynamic-update-slice_fusion.101
  59.9 0.7 constant_dynamic-update-slice_fusion.86
  62.0 0.7 constant_dynamic-update-slice_fusion.83
  70.5 0.7 constant_dynamic-update-slice_fusion.71
  74.7 0.7 constant_dynamic-update-slice_fusion.65
  88.8 0.7 constant_dynamic-update-slice_fusion.45
  117.0 0.7 constant_dynamic-update-slice_fusion.5
  119.1 0.7 constant_dynamic-update-slice_fusion.2
  119.8 0.7 constant_dynamic-update-slice_fusion.1
  120.8 0.7 constant_dynamic-update-slice_fusion
  121.6 7.2 %all-to-all-start.2 = ((s32[16,1,16]{2,1,0:T(1,128)}), s32[16,1,16]{2,1,0:T(1,128)S(1)}, u32[]{:S(2)}, u32[]{:S(2)}) async-start(s32[16,1,16]{2,1,0:T(1,128)} %bitcast.7), calls=%async_computation.2 | async-start | bytes 16384 | tf_op jit(solution)/shard_map/all_to_all | solution.py:106
  128.8 7.0 %copy.293 = bf16[128,1,4,2,128]{4,2,3,1,0:T(4,128)(2,1)} copy(bf16[128,1,4,2,128]{2,4,3,1,0:T(8,128)(2,1)} %constant_dynamic-update-slice_fusion) | data formatting | bytes 524288 | tf_op jit(solution)/shard_map/stack | solution.py:77
  136.4 7.2 %all-to-all-start.1 = ((f32[16,16,2]{1,2,0:T(2,128)}), f32[16,16,2]{1,2,0:T(2,128)S(1)}, u32[]{:S(2)}, u32[]{:S(2)}) async-start(f32[16,16,2]{1,2,0:T(2,128)} %copy.287), calls=%async_computation.1 | async-start | bytes 32768 | tf_op jit(solution)/shard_map/all_to_all | solution.py:107
  144.0 7.3 %all-to-all-done.1 = f32[16,16,2]{1,2,0:T(2,128)S(1)} async-done(((f32[16,16,2]{1,2,0:T(2,128)}), f32[16,16,2]{1,2,0:T(2,128)S(1)}, u32[]{:S(2)}, u32[]{:S(2)}) %all-to-all-start.1) | async-done | bytes 2080 | tf_op jit(solution)/shard_map/all_to_all | solution.py:107
  151.3 6.4 %all-to-all-start.3 = ((bf16[128,1,4,2,128]{4,2,3,1,0:T(4,128)(2,1)}), bf16[128,1,4,2,128]{4,2,3,1,0:T(4,128)(2,1)S(1)}, u32[]{:S(2)}, u32[]{:S(2)}) async-start(bf16[128,1,4,2,128]{4,2,3,1,0:T(4,128)(2,1)} %copy.293), calls=%async_computation.3 | async-start | bytes 524288 | tf_op jit(solution)/shard_map/all_to_all | solution.py:77
  158.2 1.3 select_reduce_fusion
  159.4 8.9 %all-to-all-done.3 = bf16[128,1,4,2,128]{4,2,3,1,0:T(4,128)(2,1)S(1)} async-done(((bf16[128,1,4,2,128]{4,2,3,1,0:T(4,128)(2,1)}), bf16[128,1,4,2,128]{4,2,3,1,0:T(4,128)(2,1)S(1)}, u32[]{:S(2)}, u32[]{:S(2)}) %all-to-all-start.3) | async-done | bytes 262176 | tf_op jit(solution)/shard_map/all_to_all | solution.py:77
  168.6 2.7 %collective-permute-start = (bf16[4,128,128]{2,1,0:T(8,128)(2,1)S(1)}, bf16[4,128,128]{2,1,0:T(8,128)(2,1)S(1)}, u32[]{:S(2)}, u32[]{:S(2)}) collective-permute-start(bf16[4,128,128]{2,1,0:T(8,128)(2,1)S(1)} %fusion.8), channel_id=1, source_target_pairs={{0,8},{8,16},{16,24},{24,32},{32,40},{40,48},{48,56},{56,64},{64,7... | collective-permute-start | bytes 393224 | tf_op jit(solution)/shard_map/ppermute | solution.py:16
  171.3 1.3 collective-permute-start.1
  173.9 4.3 %collective-permute-done.1 = bf16[4,128,128]{2,1,0:T(8,128)(2,1)S(1)} collective-permute-done((bf16[4,128,128]{2,1,0:T(8,128)(2,1)S(1)}, bf16[4,128,128]{2,1,0:T(8,128)(2,1)S(1)}, u32[]{:S(2)}, u32[]{:S(2)}) %collective-permute-start.1) | collective-permute-done | bytes 131104 | tf_op jit(solution)/shard_map/ppermute | solution.py:17
  178.6 15.0 %all_to_all.27 = f32[16,16,128]{2,1,0:T(8,128)S(1)} all-to-all(f32[16,16,128]{2,1,0:T(8,128)S(1)} %fusion.387), channel_id=1, replica_groups=mesh['ma'=16,'band'=8] {'ma'}, dimensions={0} | all-to-all | bytes 262144 | tf_op jit(solution)/shard_map/all_to_all | solution.py:121
  193.6 0.9 fusion.19
  (157 shorter events, 86.5 us)
Async XLA Ops:
  2.9 125.9 %copy-start.1 = (f32[16,16,4]{1,0,2:T(8,128)}, f32[16,16,4]{1,0,2:T(8,128)S(1)}, u32[]{:S(2)}) copy-start(f32[16,16,4]{1,0,2:T(8,128)S(1)} %reshape.275) | copy-start | bytes 12292
  3.5 118.0 %all-to-all-start = ((s32[16,1,16]{2,1,0:T(1,128)}), s32[16,1,16]{2,1,0:T(1,128)S(1)}, u32[]{:S(2)}, u32[]{:S(2)}) async-start(s32[16,1,16]{2,1,0:T(1,128)} %bitcast.4), calls=%async_computation | async-start | bytes 16384 | tf_op jit(solution)/shard_map/all_to_all | solution.py:105
  17.9 7.1 %copy-start = (bf16[1,8192,256]{1,2,0:T(8,128)(2,1)S(1)}, bf16[1,8192,256]{1,2,0:T(8,128)(2,1)}, u32[]{:S(2)}) copy-start(bf16[1,8192,256]{1,2,0:T(8,128)(2,1)} %copy.292) | copy-start | bytes 12582916
  17.9 10.6 %copy-start.3 = (bf16[1,2,8192,512]{3,2,1,0:T(8,128)(2,1)S(1)}, bf16[1,2,8192,512]{3,2,1,0:T(8,128)(2,1)}, u32[]{:S(2)}) copy-start(bf16[1,2,8192,512]{3,2,1,0:T(8,128)(2,1)} %param.8) | copy-start | bytes 50331652
  84.6 36.0 %copy-start.2 = (s32[128]{0:T(128)S(1)}, s32[128]{0:T(128)}, u32[]{:S(2)}) copy-start(s32[128]{0:T(128)} %param.9) | copy-start | bytes 1540
  121.6 14.9 %all-to-all-start.2 = ((s32[16,1,16]{2,1,0:T(1,128)}), s32[16,1,16]{2,1,0:T(1,128)S(1)}, u32[]{:S(2)}, u32[]{:S(2)}) async-start(s32[16,1,16]{2,1,0:T(1,128)} %bitcast.7), calls=%async_computation.2 | async-start | bytes 16384 | tf_op jit(solution)/shard_map/all_to_all | solution.py:106
  128.8 7.0 %slice-start = ((f32[16,16,4]{1,0,2:T(8,128)}), f32[16,16,2]{1,0,2:T(8,128)S(1)}, s32[]{:S(2)}) async-start(f32[16,16,4]{1,0,2:T(8,128)} %copy-done.1), calls=%async_computation.5 | async-start | bytes 32768 | tf_op jit(solution)/shard_map/slice | solution.py:104
  136.4 14.8 %all-to-all-start.1 = ((f32[16,16,2]{1,2,0:T(2,128)}), f32[16,16,2]{1,2,0:T(2,128)S(1)}, u32[]{:S(2)}, u32[]{:S(2)}) async-start(f32[16,16,2]{1,2,0:T(2,128)} %copy.287), calls=%async_computation.1 | async-start | bytes 32768 | tf_op jit(solution)/shard_map/all_to_all | solution.py:107
  151.3 17.1 %all-to-all-start.3 = ((bf16[128,1,4,2,128]{4,2,3,1,0:T(4,128)(2,1)}), bf16[128,1,4,2,128]{4,2,3,1,0:T(4,128)(2,1)S(1)}, u32[]{:S(2)}, u32[]{:S(2)}) async-start(bf16[128,1,4,2,128]{4,2,3,1,0:T(4,128)(2,1)} %copy.293), calls=%async_computation.3 | async-start | bytes 524288 | tf_op jit(solution)/shard_map/all_to_all | solution.py:77
  168.6 5.3 %collective-permute-start = (bf16[4,128,128]{2,1,0:T(8,128)(2,1)S(1)}, bf16[4,128,128]{2,1,0:T(8,128)(2,1)S(1)}, u32[]{:S(2)}, u32[]{:S(2)}) collective-permute-start(bf16[4,128,128]{2,1,0:T(8,128)(2,1)S(1)} %fusion.8), channel_id=1, source_target_pairs={{0,8},{8,16},{16,24},{24,32},{32,40},{40,48},{48,56},{56,64},{64,7... | collective-permute-start | bytes 393224 | tf_op jit(solution)/shard_map/ppermute | solution.py:16
  171.3 6.9 %collective-permute-start.1 = (bf16[4,128,128]{2,1,0:T(8,128)(2,1)S(1)}, bf16[4,128,128]{2,1,0:T(8,128)(2,1)S(1)}, u32[]{:S(2)}, u32[]{:S(2)}) collective-permute-start(bf16[4,128,128]{2,1,0:T(8,128)(2,1)S(1)} %fusion.8), channel_id=1, source_target_pairs={{8,0},{16,8},{24,16},{32,24},{40,32},{48,40},{56,48},{64,56},{72,6... | collective-permute-start | bytes 393224 | tf_op jit(solution)/shard_map/ppermute | solution.py:17
